TPU v7x, 512 devices: a whole 4x8x8 slice. The times are simulated.
512 devices in a mesh: req: 64 (over y, x, core), tp: 8 (over z).
Axes of the slice: x: 4, y: 8, z: 8, core: 2. Of those that a mesh axis runs over, the one named last changes fastest.
Arguments:
- tokens: bfloat16 [8192, 8192], P('req', 'tp'), may hold values from -6 to 6
- kv_weight: bfloat16 [8192, 1024], P('tp'), may hold values from -0.0625 to 0.0625
- queries: bfloat16 [8192, 4096], P('req', 'tp'), may hold values from -96 to 96, as said below
- lengths: int32 [32], replicated, may hold values from 1 to 384, 8192 in all
- page_owner: int32 [4096, 1], P('req'), may hold values from 0 to 63; in each aligned block of 64 rows (0 to 63, 64 to 127, ...) at most 2 rows name the same one
Outputs:
- attended: bfloat16 [8192, 4096], P('req', 'tp')
- cache: bfloat16 [16384, 1024], P('req', 'tp')
Inputs may be any that keep to these rules, and one draw needn't show every extreme that they name: `queries`: real values; entries of a row share a scale. The 32 lengths sum to 8192; the largest is exactly 384. `page_owner`: among the 64 pages of one device no owner is named more than 2 times, a bound that some block reaches.
All inputs are finite; a program needn't handle non-finite values.
Results may differ from a plain program's by a relative error of at most 0.012.
Values may be sent and summed in bfloat16 or wider, within the bound.
No kernel may reach another device: no remote copies, remote signals or barrier semaphores. Data moves between devices by JAX's collectives and lax.ppermute only.
A program may use at most 64 MiB of HBM per device.

v0:
```python
import math
import jax
import jax.numpy as jnp
from jax import lax
from jax.sharding import PartitionSpec as P

HD = 128
HQ = 32
KVH = 4
BACK = 3
rope_base = 500000.0


def shifted(value, axis, steps):
    count = lax.axis_size(axis)
    first, last = (max(0, -steps), min(count, count - steps))
    return lax.ppermute(value, axis, [(source, source + steps) for source in range(first, last)])


def rotate(values, positions):
    middle = HD // 2
    frequency = rope_base ** (-(2.0 * jnp.arange(middle, dtype=jnp.float32)) / HD)
    angles = positions.astype(jnp.float32)[:, None] * frequency[None, :]
    cosine = jnp.cos(angles)[:, None, :]
    sine = jnp.sin(angles)[:, None, :]
    front = values[..., :middle]
    behind = values[..., middle:]
    return jnp.concatenate(
        [front * cosine - behind * sine, behind * cosine + front * sine], axis=-1
    )


def rotate_keys(block, positions):
    rows = block.shape[0]
    parts = block.shape[1] // HD
    shaped = block.reshape(rows, parts, HD)
    turned = rotate(shaped, positions)
    is_key = jnp.arange(parts, dtype=jnp.int32) % 2 == 0
    return jnp.where(is_key[None, :, None], turned, shaped).reshape(rows, parts * HD)


def segment_info(lengths, indices):
    ends = jnp.cumsum(lengths)
    before = ends[None, :] <= indices[:, None]
    segment = jnp.sum(before.astype(jnp.int32), axis=1)
    start = jnp.sum(jnp.where(before, lengths[None, :], 0), axis=1)
    return (segment, indices - start)


def local(tokens, kv_weight, queries, lengths, page_owner):
    rows = tokens.shape[0]
    columns = kv_weight.shape[1]
    share = columns // lax.axis_size("tp")
    tp_index = lax.axis_index("tp")
    req_index = lax.axis_index("req")
    local_index = req_index * rows + jnp.arange(rows, dtype=jnp.int32)
    segment, positions = segment_info(lengths, local_index)
    local_heads = queries.shape[1] // HD
    group = HQ // KVH
    per_group = min(local_heads, group)
    kv_count = local_heads // per_group
    first_head = tp_index * local_heads // group
    partial_value = jnp.dot(tokens, kv_weight, preferred_element_type=jnp.float32)
    summed = lax.psum(partial_value, "tp")
    cache_rows = rotate_keys(summed, positions).astype(jnp.bfloat16)
    mine = lax.dynamic_slice_in_dim(cache_rows, tp_index * share, share, 1)
    near = lax.dynamic_slice_in_dim(cache_rows, first_head * 2 * HD, kv_count * 2 * HD, 1)
    rotated = rotate(queries.astype(jnp.float32).reshape(rows, local_heads, HD), positions).astype(
        jnp.bfloat16
    )
    blocks = []
    for distance in range(BACK, 0, -1):
        blocks.append(shifted(near, "req", distance))
    blocks.append(near)
    window = jnp.concatenate(blocks, axis=0)
    key_total = (BACK + 1) * rows
    key_index = (req_index - BACK) * rows + jnp.arange(key_total, dtype=jnp.int32)
    key_segment, unused = segment_info(lengths, key_index)
    allowed = (
        (key_index[None, :] >= 0)
        & (key_index[None, :] <= local_index[:, None])
        & (key_segment[None, :] == segment[:, None])
    )
    key_parts = window.reshape(key_total, kv_count, 2, HD)
    head_keys = jnp.transpose(key_parts[:, :, 0, :], (1, 0, 2))
    head_values = jnp.transpose(key_parts[:, :, 1, :], (1, 0, 2))
    query_heads = jnp.transpose(rotated, (1, 0, 2))

    def attend_head(head):
        query_head = query_heads[head]
        slot = head // per_group
        key_head = head_keys[slot]
        value_head = head_values[slot]
        scores = lax.dot_general(
            query_head, key_head, (((1,), (1,)), ((), ())), preferred_element_type=jnp.float32
        ) / math.sqrt(HD)
        scores = jnp.where(allowed, scores, -1e30)
        largest = jnp.max(scores, axis=1, keepdims=True)
        weights = jnp.exp(scores - largest)
        total = jnp.sum(weights, axis=1, keepdims=True)
        mixed = jnp.dot(
            weights.astype(jnp.bfloat16), value_head, preferred_element_type=jnp.float32
        )
        return (mixed / total).astype(jnp.bfloat16)

    outputs = lax.map(attend_head, jnp.arange(local_heads, dtype=jnp.int32))
    attended = jnp.transpose(outputs, (1, 0, 2)).reshape(rows, local_heads * HD)
    pages_here = page_owner.shape[0]
    owners = page_owner[:, 0]
    page_rows = rows // pages_here
    capacity = 2 * pages_here // lax.axis_size("req")
    order = jnp.arange(pages_here, dtype=jnp.int32)
    earlier = (owners[:, None] == owners[None, :]) & (order[None, :] < order[:, None])
    rank = jnp.sum(earlier.astype(jnp.int32), axis=1)
    target = owners * capacity + rank
    slots = lax.axis_size("req") * capacity
    placing = (jnp.arange(slots, dtype=jnp.int32)[:, None] == target[None, :]).astype(jnp.bfloat16)
    paged = mine.reshape(pages_here, page_rows * share)
    outgoing = jnp.dot(placing, paged, preferred_element_type=jnp.float32).astype(jnp.bfloat16)
    incoming = lax.all_to_all(outgoing, "req", split_axis=0, concat_axis=0, tiled=True)
    cache = incoming.reshape(slots * page_rows, share)
    return (attended, cache)


def solution(mesh):
    in_specs = (P("req", "tp"), P("tp", None), P("req", "tp"), P(), P("req", None))
    out_specs = (P("req", "tp"), P("req", "tp"))
    return jax.shard_map(local, mesh=mesh, in_specs=in_specs, out_specs=out_specs, check_vma=False)
```

profile of v0, /device:TPU:1, one launch (start us, length us, event | category | flops | bytes accessed | tf_op | source)
XLA Modules:
  0.0 141.3 jit_solution(10183100208050448432)
XLA Ops:
  7.2 0.0 copy-start
  7.2 0.0 copy-start.3
  7.2 0.0 copy-start.2
  7.2 0.0 copy-start.4
  7.2 0.0 all-reduce.2.cloned.1.call-start
  7.3 1.5 %copy-done = bf16[1024,1024]{1,0:T(8,128)(2,1)S(1)} copy-done((bf16[1024,1024]{1,0:T(8,128)(2,1)S(1)}, bf16[1024,1024]{1,0:T(8,128)(2,1)}, u32[]{:S(2)}) %copy-start) | copy-done | bytes 2097176
  8.8 2.2 %fusion.23 = f32[128,1024]{1,0:T(8,128)} fusion(bf16[128,1024]{1,0:T(8,128)(2,1)} %param.7, bf16[1024,1024]{1,0:T(8,128)(2,1)S(1)} %copy-done), kind=kOutput, calls=%fused_computation.54 | convolution fusion | flops 268435456 | bytes 2883584 | tf_op jit(solution)/shard_map/dot_general | solution.py:63
  11.0 0.0 all-reduce.2.cloned.1.call-update
  11.1 0.0 copy-done.3
  11.1 0.1 copy.20
  11.2 0.1 reduce-window.8
  11.2 0.1 reduce
  11.3 0.1 fusion.19
  11.5 0.2 multiply_cosine_fusion
  11.7 0.1 copy.21
  11.8 0.1 copy.22
  11.9 0.0 copy-done.2
  11.9 0.1 copy.19
  12.1 0.1 convert_reduce_fusion
  12.2 0.0 copy-done.4
  12.2 0.2 convert_reduce_fusion.1
  12.4 0.1 broadcast_bitcast_fusion
  12.5 79.8 %all-reduce.2.cloned.1.call-done = f32[128,1024]{1,0:T(8,128)} async-done(((f32[128,1024]{1,0:T(8,128)}), f32[128,1024]{1,0:T(8,128)}) %all-reduce.2.cloned.1.call-update) | async-done | bytes 524304 | tf_op jit(solution)/shard_map/psum | solution.py:64
  92.2 0.0 copy-start.1
  92.2 1.2 copy.31
  93.5 0.3 multiply_subtract_fusion
  93.7 0.1 pad_maximum_fusion
  93.9 0.0 copy-done.1
  93.9 0.1 fusion.15
  94.0 9.6 %collective-permute-start = (bf16[128,256]{1,0:T(8,128)(2,1)S(1)}, bf16[128,256]{1,0:T(8,128)(2,1)S(1)}, u32[]{:S(2)}, u32[]{:S(2)}) collective-permute-start(bf16[128,256]{1,0:T(8,128)(2,1)S(1)} %constant_dynamic-slice_fusion.1), channel_id=1, source_target_pairs={{0,24},{8,32},{16,40},{24,48},{32,56},{40,64},{48,72},{56,80},{64,... | collective-permute-start | bytes 196616 | tf_op jit(solution)/shard_map/ppermute | solution.py:17
  103.6 2.2 %collective-permute-start.1 = (bf16[128,256]{1,0:T(8,128)(2,1)S(1)}, bf16[128,256]{1,0:T(8,128)(2,1)S(1)}, u32[]{:S(2)}, u32[]{:S(2)}) collective-permute-start(bf16[128,256]{1,0:T(8,128)(2,1)S(1)} %constant_dynamic-slice_fusion.1), channel_id=1, source_target_pairs={{0,16},{8,24},{16,32},{24,40},{32,48},{40,56},{48,64},{56,72},{64,... | collective-permute-start | bytes 196616 | tf_op jit(solution)/shard_map/ppermute | solution.py:17
  105.8 1.9 %collective-permute-start.2 = (bf16[128,256]{1,0:T(8,128)(2,1)S(1)}, bf16[128,256]{1,0:T(8,128)(2,1)S(1)}, u32[]{:S(2)}, u32[]{:S(2)}) collective-permute-start(bf16[128,256]{1,0:T(8,128)(2,1)S(1)} %constant_dynamic-slice_fusion.1), channel_id=1, source_target_pairs={{0,8},{8,16},{16,24},{24,32},{32,40},{40,48},{48,56},{56,64},{64,7... | collective-permute-start | bytes 196616 | tf_op jit(solution)/shard_map/ppermute | solution.py:17
  107.7 0.1 convolution_convert_fusion
  107.9 0.7 all_to_all.6
  108.6 9.9 %all-to-all-start = ((bf16[64,2,256]{2,1,0:T(2,128)(2,1)}), bf16[64,2,256]{2,1,0:T(2,128)(2,1)S(1)}, u32[]{:S(2)}, u32[]{:S(2)}) async-start(bf16[64,2,256]{2,1,0:T(2,128)(2,1)} %all_to_all.6), calls=%async_computation | async-start | bytes 131072 | tf_op jit(solution)/shard_map/all_to_all | solution.py:120
  118.5 0.0 collective-permute-done
  118.5 0.0 collective-permute-done.1
  118.5 0.0 collective-permute-done.2
  118.5 0.1 reshape.160
  118.6 0.4 fusion.22
  119.0 14.1 %while.11 = (s32[]{:T(128)}, bf16[4,128,128]{2,1,0:T(8,128)(2,1)S(1)}, s32[4]{0:T(128)S(1)}, bf16[4,128,128]{1,2,0:T(8,128)(2,1)S(1)}, bf16[1,512,128]{2,1,0:T(8...) while((s32[]{:T(128)}, ...), condition=%wide.region_8.9_spmd.clone, body=%wide.region_5.8_spmd.clone.sunk | while | flops 34307844 | bytes 1122491 | solution.py:106
  119.1 0.7 dynamic_slice.30
  121.8 0.3 fusion.35
  122.1 0.2 fusion.36
  122.3 0.3 fusion.37
  122.6 0.7 dynamic_slice.30
  125.3 0.3 fusion.35
  125.6 0.2 fusion.36
  125.8 0.3 fusion.37
  126.1 0.7 dynamic_slice.30
  128.8 0.3 fusion.35
  129.1 0.2 fusion.36
  129.3 0.3 fusion.37
  129.6 0.7 dynamic_slice.30
  132.4 0.3 fusion.35
  132.7 0.2 fusion.36
  132.9 0.3 fusion.37
  133.1 0.7 copy_bitcast_fusion
  133.8 0.0 all-to-all-done
  133.8 0.7 reshape.163
  (17 shorter events, 0.2 us)
Async XLA Ops:
  7.2 1.6 %copy-start = (bf16[1024,1024]{1,0:T(8,128)(2,1)S(1)}, bf16[1024,1024]{1,0:T(8,128)(2,1)}, u32[]{:S(2)}) copy-start(bf16[1024,1024]{1,0:T(8,128)(2,1)} %param.8) | copy-start | bytes 6291460
  7.2 3.9 %copy-start.3 = (s32[32]{0:T(128)S(1)}, s32[32]{0:T(128)}, u32[]{:S(2)}) copy-start(s32[32]{0:T(128)} %param.10) | copy-start | bytes 388
  7.2 4.7 %copy-start.2 = (bf16[128,512]{1,0:T(8,128)(2,1)S(1)}, bf16[128,512]{1,0:T(8,128)(2,1)}, u32[]{:S(2)}) copy-start(bf16[128,512]{1,0:T(8,128)(2,1)} %param.9) | copy-start | bytes 393220
  7.2 5.0 %copy-start.4 = (s32[64,1]{0,1:T(1,128)S(1)}, s32[64,1]{0,1:T(1,128)}, u32[]{:S(2)}) copy-start(s32[64,1]{0,1:T(1,128)} %param.11) | copy-start | bytes 772
  7.2 85.0 %all-reduce.2.cloned.1.call-start = ((), (), s32[]{:S(2)}) async-start(), calls=%async_computation.1 | async-start | bytes 1048576 | tf_op jit(solution)/shard_map/psum | solution.py:64
  92.2 1.6 %copy-start.1 = (f32[128,1024]{1,0:T(8,128)S(1)}, f32[128,1024]{1,0:T(8,128)}, u32[]{:S(2)}) copy-start(f32[128,1024]{1,0:T(8,128)} %all-reduce.2.cloned.1.call-done) | copy-start | bytes 1572868
  94.0 24.5 %collective-permute-start = (bf16[128,256]{1,0:T(8,128)(2,1)S(1)}, bf16[128,256]{1,0:T(8,128)(2,1)S(1)}, u32[]{:S(2)}, u32[]{:S(2)}) collective-permute-start(bf16[128,256]{1,0:T(8,128)(2,1)S(1)} %constant_dynamic-slice_fusion.1), channel_id=1, source_target_pairs={{0,24},{8,32},{16,40},{24,48},{32,56},{40,64},{48,72},{56,80},{64,... | collective-permute-start | bytes 196616 | tf_op jit(solution)/shard_map/ppermute | solution.py:17
  103.6 14.9 %collective-permute-start.1 = (bf16[128,256]{1,0:T(8,128)(2,1)S(1)}, bf16[128,256]{1,0:T(8,128)(2,1)S(1)}, u32[]{:S(2)}, u32[]{:S(2)}) collective-permute-start(bf16[128,256]{1,0:T(8,128)(2,1)S(1)} %constant_dynamic-slice_fusion.1), channel_id=1, source_target_pairs={{0,16},{8,24},{16,32},{24,40},{32,48},{40,56},{48,64},{56,72},{64,... | collective-permute-start | bytes 196616 | tf_op jit(solution)/shard_map/ppermute | solution.py:17
  105.8 12.7 %collective-permute-start.2 = (bf16[128,256]{1,0:T(8,128)(2,1)S(1)}, bf16[128,256]{1,0:T(8,128)(2,1)S(1)}, u32[]{:S(2)}, u32[]{:S(2)}) collective-permute-start(bf16[128,256]{1,0:T(8,128)(2,1)S(1)} %constant_dynamic-slice_fusion.1), channel_id=1, source_target_pairs={{0,8},{8,16},{16,24},{24,32},{32,40},{40,48},{48,56},{56,64},{64,7... | collective-permute-start | bytes 196616 | tf_op jit(solution)/shard_map/ppermute | solution.py:17
  108.6 25.2 %all-to-all-start = ((bf16[64,2,256]{2,1,0:T(2,128)(2,1)}), bf16[64,2,256]{2,1,0:T(2,128)(2,1)S(1)}, u32[]{:S(2)}, u32[]{:S(2)}) async-start(bf16[64,2,256]{2,1,0:T(2,128)(2,1)} %all_to_all.6), calls=%async_computation | async-start | bytes 131072 | tf_op jit(solution)/shard_map/all_to_all | solution.py:120
Sparse Core Ops, SparseCore 0:
  11.1 81.0 all-reduce.1
where the time goes:
time: 142 us; the launch traced here: 141 us
  waiting for transfers between devices  79.8 us (56%)
  starting transfers between devices  23.6 us (17%)
  between operations  14.4 us (10%)
  local copies, waits for them, and re-layouts  8.42 us (6%)
  loops' own time  8.37 us (6%)
  matrix products  4.61 us (3%)
  other arithmetic  2.13 us (2%)
    psum x1, waiting for transfers between devices, local(): summed = lax.psum(partial_value, 'tp')  79.8 us
    ppermute x3, starting transfers between devices, shifted(): lax.ppermute(value, axis, [(source, source + steps) for source in range(f...  13.7 us
    all_to_all x1, starting transfers between devices, local(): lax.all_to_all(outgoing, 'req', split_axis=0, concat_axis=0, tiled=True)  9.92 us
    another operation x1, loops' own time, local(): outputs = lax.map(attend_head, jnp.arange(local_heads, dtype=jnp.int32))  8.37 us
    unnamed x12, local copies, waits for them, and re-layouts  2.86 us
  transfers between devices with their start and end apart: 5, of which 1 were waited for; matrix products, arithmetic and copies ran while one was open for 6% of the time, Pallas kernels for 0%

commit v1 on v0

--- a/solution.py
+++ b/solution.py
@@ -1,3 +1,4 @@
+import functools
 import math
 import jax
 import jax.numpy as jnp
@@ -9,6 +10,13 @@
 KVH = 4
 BACK = 3
 rope_base = 500000.0
+
+
+def read_matrix(piece_in, axis_key):
+    return jax.lax.all_gather(piece_in, axis_key).sum(axis=0)
+
+
+floor_settle = functools.partial(read_matrix, axis_key="tp")
 
 
 def shifted(value, axis, steps):
@@ -61,7 +69,7 @@
     kv_count = local_heads // per_group
     first_head = tp_index * local_heads // group
     partial_value = jnp.dot(tokens, kv_weight, preferred_element_type=jnp.float32)
-    summed = lax.psum(partial_value, "tp")
+    summed = floor_settle(partial_value)
     cache_rows = rotate_keys(summed, positions).astype(jnp.bfloat16)
     mine = lax.dynamic_slice_in_dim(cache_rows, tp_index * share, share, 1)
     near = lax.dynamic_slice_in_dim(cache_rows, first_head * 2 * HD, kv_count * 2 * HD, 1)

time: 142 us -> 121 us (0.85)
  waiting for transfers between devices: 79.8 us -> 62.2 us
  starting transfers between devices: 23.6 us -> 19.4 us
  other arithmetic: 2.13 us -> 4.74 us
    psum x1 -> x0, waiting for transfers between devices: 79.8 us -> none  [local(): summed = lax.psum(partial_value, 'tp')]
    all_gather x0 -> x1, waiting for transfers between devices: none -> 62.2 us  [read_matrix(): return jax.lax.all_gather(piece_in, axis_key).sum(axis=0)]
    ppermute x3, starting transfers between devices: 13.7 us -> 9.56 us  [shifted(): lax.ppermute(value, axis, [(source, source + steps) for source in range(f...]
    reduce_sum x0 -> x1, other arithmetic: none -> 2.61 us  [read_matrix(): return jax.lax.all_gather(piece_in, axis_key).sum(axis=0)]
  transfers between devices with their start and end apart: 5 -> 5, of which waited for: 1 -> 1; matrix products, arithmetic and copies ran while one was open for 6% -> 7% of each run, Pallas kernels for 0% -> 0%
where the time goes in v1:
time: 121 us
  waiting for transfers between devices  62.2 us (51%)
  starting transfers between devices  19.4 us (16%)
  between operations  14.4 us (12%)
  loops' own time  8.37 us (7%)
  local copies, waits for them, and re-layouts  7.23 us (6%)
  other arithmetic  4.74 us (4%)
  matrix products  4.59 us (4%)
    all_gather x1, waiting for transfers between devices, read_matrix(): return jax.lax.all_gather(piece_in, axis_key).sum(axis=0)  62.2 us
    all_to_all x1, starting transfers between devices, local(): lax.all_to_all(outgoing, 'req', split_axis=0, concat_axis=0, tiled=True)  9.81 us
    ppermute x3, starting transfers between devices, shifted(): lax.ppermute(value, axis, [(source, source + steps) for source in range(f...  9.56 us
    another operation x1, loops' own time, local(): outputs = lax.map(attend_head, jnp.arange(local_heads, dtype=jnp.int32))  8.37 us
    dynamic_slice x4, local copies, waits for them, and re-layouts, local(): outputs = lax.map(attend_head, jnp.arange(local_heads, dtype=jnp.int32))  2.67 us
    reduce_sum x1, other arithmetic, read_matrix(): return jax.lax.all_gather(piece_in, axis_key).sum(axis=0)  2.61 us
  transfers between devices with their start and end apart: 5, of which 1 were waited for; matrix products, arithmetic and copies ran while one was open for 7% of the time, Pallas kernels for 0%

profile of v1, /device:TPU:1, one launch (start us, length us, event | category | flops | bytes accessed | tf_op | source)
XLA Modules:
  0.0 120.9 jit_solution(12185984456571214890)
XLA Ops:
  7.2 0.0 copy-start
  7.2 0.0 copy-start.2
  7.2 0.0 copy-start.1
  7.2 0.0 copy-start.3
  7.2 0.0 all-gather.3.cloned.1.call-start
  7.3 1.5 %copy-done = bf16[1024,1024]{1,0:T(8,128)(2,1)S(1)} copy-done((bf16[1024,1024]{1,0:T(8,128)(2,1)S(1)}, bf16[1024,1024]{1,0:T(8,128)(2,1)}, u32[]{:S(2)}) %copy-start) | copy-done | bytes 2097176
  8.8 2.2 %fusion.22 = f32[128,1024]{1,0:T(8,128)} fusion(bf16[128,1024]{1,0:T(8,128)(2,1)} %param.7, bf16[1024,1024]{1,0:T(8,128)(2,1)S(1)} %copy-done), kind=kOutput, calls=%fused_computation.53 | convolution fusion | flops 268435456 | bytes 2883584 | tf_op jit(solution)/shard_map/dot_general | solution.py:71
  11.0 0.0 all-gather.3.cloned.1.call-update
  11.0 0.0 copy-done.2
  11.0 0.1 copy.32
  11.1 0.1 reduce-window.8
  11.2 0.1 reduce
  11.3 0.1 fusion.19
  11.4 0.2 multiply_cosine_fusion
  11.6 0.1 copy.33
  11.7 0.1 copy.34
  11.8 0.0 copy-done.1
  11.8 0.1 copy.31
  12.0 0.0 copy-done.3
  12.0 0.2 convert_reduce_fusion.1
  12.2 0.1 convert_reduce_fusion
  12.4 0.1 broadcast_bitcast_fusion
  12.5 62.2 %all-gather.3.cloned.1.call-done = f32[1024,1024]{1,0:T(8,128)} async-done(((f32[128,1024]{1,0:T(8,128)}), f32[1024,1024]{1,0:T(8,128)}) %all-gather.3.cloned.1.call-update) | async-done | bytes 4194320 | tf_op jit(solution)/shard_map/all_gather | solution.py:16
  74.6 2.6 %reduce_sum.55 = f32[128,1024]{1,0:T(8,128)S(1)} reduce(f32[8,128,1024]{2,1,0:T(8,128)} %bitcast.62, f32[]{:T(128)} %constant.85.clone.1), dimensions={0}, to_apply=%region_2.3 | reduce | flops 917504 | bytes 4718596 | tf_op jit(solution)/shard_map/reduce_sum | solution.py:16
  77.2 0.1 copy.42
  77.3 0.3 multiply_subtract_fusion
  77.6 0.1 pad_maximum_fusion
  77.8 0.1 fusion.15
  77.9 5.3 %collective-permute-start = (bf16[128,256]{1,0:T(8,128)(2,1)S(1)}, bf16[128,256]{1,0:T(8,128)(2,1)S(1)}, u32[]{:S(2)}, u32[]{:S(2)}) collective-permute-start(bf16[128,256]{1,0:T(8,128)(2,1)S(1)} %constant_dynamic-slice_fusion.1), channel_id=1, source_target_pairs={{0,24},{8,32},{16,40},{24,48},{32,56},{40,64},{48,72},{56,80},{64,... | collective-permute-start | bytes 196616 | tf_op jit(solution)/shard_map/ppermute | solution.py:25
  83.2 2.2 %collective-permute-start.1 = (bf16[128,256]{1,0:T(8,128)(2,1)S(1)}, bf16[128,256]{1,0:T(8,128)(2,1)S(1)}, u32[]{:S(2)}, u32[]{:S(2)}) collective-permute-start(bf16[128,256]{1,0:T(8,128)(2,1)S(1)} %constant_dynamic-slice_fusion.1), channel_id=1, source_target_pairs={{0,16},{8,24},{16,32},{24,40},{32,48},{40,56},{48,64},{56,72},{64,... | collective-permute-start | bytes 196616 | tf_op jit(solution)/shard_map/ppermute | solution.py:25
  85.4 2.0 %collective-permute-start.2 = (bf16[128,256]{1,0:T(8,128)(2,1)S(1)}, bf16[128,256]{1,0:T(8,128)(2,1)S(1)}, u32[]{:S(2)}, u32[]{:S(2)}) collective-permute-start(bf16[128,256]{1,0:T(8,128)(2,1)S(1)} %constant_dynamic-slice_fusion.1), channel_id=1, source_target_pairs={{0,8},{8,16},{16,24},{24,32},{32,40},{40,48},{48,56},{56,64},{64,7... | collective-permute-start | bytes 196616 | tf_op jit(solution)/shard_map/ppermute | solution.py:25
  87.5 0.1 convolution_convert_fusion
  87.6 0.7 all_to_all.6
  88.3 9.8 %all-to-all-start = ((bf16[64,2,256]{2,1,0:T(2,128)(2,1)}), bf16[64,2,256]{2,1,0:T(2,128)(2,1)S(1)}, u32[]{:S(2)}, u32[]{:S(2)}) async-start(bf16[64,2,256]{2,1,0:T(2,128)(2,1)} %all_to_all.6), calls=%async_computation | async-start | bytes 131072 | tf_op jit(solution)/shard_map/all_to_all | solution.py:128
  98.1 0.0 collective-permute-done
  98.1 0.0 collective-permute-done.1
  98.2 0.0 collective-permute-done.2
  98.2 0.1 copy.35
  98.4 0.1 copy.37
  98.5 0.1 copy.38
  98.6 14.1 %while.11 = (s32[]{:T(128)}, bf16[4,128,128]{2,1,0:T(8,128)(2,1)S(1)}, s32[4]{0:T(128)S(1)}, bf16[4,128,128]{1,2,0:T(8,128)(2,1)S(1)}, bf16[1,512,128]{2,1,0:T(8...) while((s32[]{:T(128)}, ...), condition=%wide.region_8.9_spmd.clone, body=%wide.region_5.8_spmd.clone.sunk | while | flops 34307844 | bytes 1122491 | solution.py:114
  98.6 0.7 dynamic_slice.30
  101.4 0.3 fusion.34
  101.7 0.2 fusion.35
  101.9 0.3 fusion.36
  102.2 0.7 dynamic_slice.30
  104.9 0.3 fusion.34
  105.2 0.2 fusion.35
  105.4 0.3 fusion.36
  105.7 0.7 dynamic_slice.30
  108.4 0.3 fusion.34
  108.7 0.2 fusion.35
  108.9 0.3 fusion.36
  109.2 0.7 dynamic_slice.30
  111.9 0.3 fusion.34
  112.2 0.2 fusion.35
  112.4 0.3 fusion.36
  112.7 0.7 copy_bitcast_fusion
  113.4 0.0 all-to-all-done
  113.4 0.7 reshape.163
  (17 shorter events, 0.2 us)
Async XLA Ops:
  7.2 1.6 %copy-start = (bf16[1024,1024]{1,0:T(8,128)(2,1)S(1)}, bf16[1024,1024]{1,0:T(8,128)(2,1)}, u32[]{:S(2)}) copy-start(bf16[1024,1024]{1,0:T(8,128)(2,1)} %param.8) | copy-start | bytes 6291460
  7.2 3.8 %copy-start.2 = (s32[32]{0:T(128)S(1)}, s32[32]{0:T(128)}, u32[]{:S(2)}) copy-start(s32[32]{0:T(128)} %param.10) | copy-start | bytes 388
  7.2 4.6 %copy-start.1 = (bf16[128,512]{1,0:T(8,128)(2,1)S(1)}, bf16[128,512]{1,0:T(8,128)(2,1)}, u32[]{:S(2)}) copy-start(bf16[128,512]{1,0:T(8,128)(2,1)} %param.9) | copy-start | bytes 393220
  7.2 4.8 %copy-start.3 = (s32[64,1]{0,1:T(1,128)S(1)}, s32[64,1]{0,1:T(1,128)}, u32[]{:S(2)}) copy-start(s32[64,1]{0,1:T(1,128)} %param.11) | copy-start | bytes 772
  7.2 67.4 %all-gather.3.cloned.1.call-start = ((), (), s32[]{:S(2)}) async-start(), calls=%async_computation.1 | async-start | bytes 4718592 | tf_op jit(solution)/shard_map/all_gather | solution.py:16
  77.9 20.3 %collective-permute-start = (bf16[128,256]{1,0:T(8,128)(2,1)S(1)}, bf16[128,256]{1,0:T(8,128)(2,1)S(1)}, u32[]{:S(2)}, u32[]{:S(2)}) collective-permute-start(bf16[128,256]{1,0:T(8,128)(2,1)S(1)} %constant_dynamic-slice_fusion.1), channel_id=1, source_target_pairs={{0,24},{8,32},{16,40},{24,48},{32,56},{40,64},{48,72},{56,80},{64,... | collective-permute-start | bytes 196616 | tf_op jit(solution)/shard_map/ppermute | solution.py:25
  83.2 14.9 %collective-permute-start.1 = (bf16[128,256]{1,0:T(8,128)(2,1)S(1)}, bf16[128,256]{1,0:T(8,128)(2,1)S(1)}, u32[]{:S(2)}, u32[]{:S(2)}) collective-permute-start(bf16[128,256]{1,0:T(8,128)(2,1)S(1)} %constant_dynamic-slice_fusion.1), channel_id=1, source_target_pairs={{0,16},{8,24},{16,32},{24,40},{32,48},{40,56},{48,64},{56,72},{64,... | collective-permute-start | bytes 196616 | tf_op jit(solution)/shard_map/ppermute | solution.py:25
  85.4 12.7 %collective-permute-start.2 = (bf16[128,256]{1,0:T(8,128)(2,1)S(1)}, bf16[128,256]{1,0:T(8,128)(2,1)S(1)}, u32[]{:S(2)}, u32[]{:S(2)}) collective-permute-start(bf16[128,256]{1,0:T(8,128)(2,1)S(1)} %constant_dynamic-slice_fusion.1), channel_id=1, source_target_pairs={{0,8},{8,16},{16,24},{24,32},{32,40},{40,48},{48,56},{56,64},{64,7... | collective-permute-start | bytes 196616 | tf_op jit(solution)/shard_map/ppermute | solution.py:25
  88.3 25.1 %all-to-all-start = ((bf16[64,2,256]{2,1,0:T(2,128)(2,1)}), bf16[64,2,256]{2,1,0:T(2,128)(2,1)S(1)}, u32[]{:S(2)}, u32[]{:S(2)}) async-start(bf16[64,2,256]{2,1,0:T(2,128)(2,1)} %all_to_all.6), calls=%async_computation | async-start | bytes 131072 | tf_op jit(solution)/shard_map/all_to_all | solution.py:128
Sparse Core Ops, SparseCore 0:
  11.1 63.4 all-gather.2
